TPU v7x, 512 devices: a whole 4x4x16 slice. The times are simulated.
512 devices in a mesh: node: 64 (over z, x), local: 8 (over y, core).
Axes of the slice: x: 4, y: 4, z: 16, core: 2. Of those that a mesh axis runs over, the one named last changes fastest.
Arguments:
- grad_out: bfloat16 [8192, 7168], P('node', 'local'), may hold values from -6 to 6
- probs: bfloat16 [8192, 8], P('node'), may hold values from 0.099609375 to 2.5
- node_list: int32 [8192, 4], P('node'), may hold values from 0 to 63, all different within a row; in each aligned block of 128 rows (0 to 127, 128 to 255, ...) at most 12 rows name the same one
- weight_down: bfloat16 [128, 1024, 7168], P('node', 'local'), may hold values from -0.1875 to 0.1875
- saved_hidden: bfloat16 [128, 768, 1024], P('node', None, 'local'), may hold values from -0.1875 to 0.1875
Outputs:
- grad_hidden: bfloat16 [128, 768, 1024], P('node', None, 'local')
- grad_probs: float32 [8192, 8], P('node')
Inputs may be any that keep to these rules, and one draw needn't show every extreme that they name: `node_list`: each token lists 4 different nodes. Among the 128 tokens of one index of node, at most 12 list any one node, and some node is listed by exactly 12 of them.
All inputs are finite; a program needn't handle non-finite values.
Results may differ from a plain program's by a relative error of at most 0.001.
Values may be sent and summed in bfloat16 or wider, within the bound.
No kernel may reach another device: no remote copies, remote signals or barrier semaphores. Data moves between devices by JAX's collectives and lax.ppermute only.
A program may use at most 128 MiB of HBM per device.

v0:
```python
import jax
import jax.numpy as jnp
from jax import lax
from jax.sharding import PartitionSpec as P


def gather_slots(source, source_row, slot_valid):
    padded = jnp.concatenate([source, jnp.zeros((1, source.shape[1]), source.dtype)], axis=0)
    index = jnp.where(slot_valid, source_row, source.shape[0])
    return jnp.take(padded, index, axis=0)


def on_device(grad_out, probs, node_list, weight_down, saved_hidden):
    node_count = lax.axis_size("node")
    tok_rows = node_list.shape[0]
    route_count = node_list.shape[1]
    slot_rows = saved_hidden.shape[1]
    capacity = slot_rows // node_count
    expert_count = weight_down.shape[0]
    node_ids = lax.broadcasted_iota(jnp.int32, (tok_rows, route_count, node_count), 2)
    listed = (node_list[:, :, None] == node_ids).astype(jnp.float32)
    member = jnp.sum((node_list[:, :, None] == node_ids).astype(jnp.int32), axis=1)
    arrival = jnp.cumsum(member, axis=0) - member
    positions = lax.broadcasted_iota(jnp.int32, (tok_rows, node_count, capacity), 2)
    select_mask = (arrival[:, :, None] == positions) & (member[:, :, None] == 1)
    select_count = select_mask.astype(jnp.int32)
    token_iota = lax.broadcasted_iota(jnp.int32, (tok_rows, node_count, capacity), 0)
    source_row = jnp.sum(select_count * token_iota, axis=0)
    slot_valid = jnp.sum(select_count, axis=0) > 0
    select_full = select_mask.astype(jnp.float32)
    grouped = probs.reshape(tok_rows, route_count, expert_count).astype(jnp.float32)
    picked = jnp.einsum("tjm,tjc->tmc", listed, grouped, precision=lax.Precision.HIGHEST)
    prob_send = jnp.einsum(
        "tms,tmc->msc", select_full, picked, precision=lax.Precision.HIGHEST
    ).astype(jnp.bfloat16)
    full_rows = lax.all_gather(grad_out, "local", axis=1, tiled=True)
    rows_send = gather_slots(full_rows, source_row, slot_valid)
    rows_in, prob_in = (
        lax.all_to_all(rows_send, "node", split_axis=0, concat_axis=0, tiled=True),
        lax.all_to_all(prob_send, "node", split_axis=0, concat_axis=0, tiled=True),
    )
    hidden_grads = jnp.einsum(
        "rd,ehd->erh",
        rows_in.reshape(slot_rows, -1),
        weight_down,
        preferred_element_type=jnp.float32,
    )
    scales = jnp.transpose(prob_in.reshape(slot_rows, expert_count).astype(jnp.float32))
    grad_hidden = (scales[:, :, None] * hidden_grads).astype(jnp.bfloat16)
    partial_value = jnp.sum(saved_hidden.astype(jnp.float32) * hidden_grads, axis=2)
    partial_value = jnp.transpose(partial_value).reshape(node_count, capacity, expert_count)
    summed = lax.psum(partial_value, "local")
    returned = lax.all_to_all(summed, "node", split_axis=0, concat_axis=0, tiled=True)
    per_node = jnp.einsum("tms,msc->tmc", select_full, returned, precision=lax.Precision.HIGHEST)
    grad_probs = jnp.einsum("tjm,tmc->tjc", listed, per_node, precision=lax.Precision.HIGHEST)
    return (grad_hidden, grad_probs.reshape(tok_rows, route_count * expert_count))


def solution(mesh):
    return jax.shard_map(
        on_device,
        mesh=mesh,
        in_specs=(
            P("node", "local"),
            P("node", None),
            P("node", None),
            P("node", "local", None),
            P("node", None, "local"),
        ),
        out_specs=(P("node", None, "local"), P("node", None)),
        check_vma=False,
    )
```

profile of v0, /device:TPU:2, one launch (start us, length us, event | category | flops | bytes accessed | tf_op | source)
XLA Modules:
  0.0 822.8 jit_solution(14254876430797097274)
XLA Ops:
  7.2 0.7 all-gather.2.cloned.1.call-update
  7.9 0.8 copy.55
  9.3 0.8 copy.58
  10.1 0.3 fusion.6
  10.6 1.2 convolution_convert_fusion
  11.8 18.6 %all-to-all-start = ((bf16[64,12,2]{1,2,0:T(2,128)(2,1)}), bf16[64,12,2]{1,2,0:T(2,128)(2,1)S(1)}, u32[]{:S(2)}, u32[]{:S(2)}) async-start(bf16[64,12,2]{1,2,0:T(2,128)(2,1)} %convolution_convert_fusion), calls=%async_computation | async-start | bytes 65536 | tf_op jit(solution)/shard_map/all_to_all | solution.py:40
  30.4 2.2 convert_reduce_fusion
  32.8 14.6 %all-gather.2.cloned.1.call-done = bf16[128,7168]{1,0:T(8,128)(2,1)} async-done(((bf16[128,896]{1,0:T(8,128)(2,1)}), bf16[128,7168]{1,0:T(8,128)(2,1)}) %all-gather.2.cloned.1.call-update) | async-done | bytes 1835024 | tf_op jit(solution)/shard_map/all_gather | solution.py:36
  47.4 1.7 concatenate.3
  49.1 9.5 %gather_fusion = bf16[768,7168]{1,0:T(8,128)(2,1)} fusion(bf16[129,7168]{1,0:T(8,128)(2,1)S(1)} %concatenate.3, s32[1024]{0:T(1024)S(1)} %pad_clamp_fusion), kind=kCustom, calls=%fused_computation | custom fusion | bytes 22023168 | tf_op jit(solution)/shard_map/jit(_take)/gather | solution.py:10
  58.5 15.4 %reshape.73 = bf16[64,12,7168]{2,1,0:T(8,128)(2,1)} reshape(bf16[768,7168]{1,0:T(8,128)(2,1)} %gather_fusion) | data formatting | bytes 22020096 | tf_op jit(solution)/shard_map/jit(_take)/gather | solution.py:10
  73.9 13.6 %broadcast_select_fusion = bf16[64,12,7168]{2,1,0:T(8,128)(2,1)} fusion(bf16[64,12,7168]{2,1,0:T(8,128)(2,1)} %reshape.73, pred[64,12]{1,0:T(8,128)(4,1)S(1)} %compare_and_fusion), kind=kLoop, calls=%fused_computation.1 | loop fusion | flops 5505024 | bytes 22020864 | tf_op jit(solution)/shard_map/jit(_take)/select_n | solution.py:10
  87.5 16.0 %all-to-all-start.1 = ((bf16[64,12,7168]{2,1,0:T(8,128)(2,1)}), bf16[64,12,7168]{2,1,0:T(8,128)(2,1)}, u32[]{:S(2)}, u32[]{:S(2)}) async-start(bf16[64,12,7168]{2,1,0:T(8,128)(2,1)} %broadcast_select_fusion), calls=%async_computation.1 | async-start | bytes 29360128 | tf_op jit(solution)/shard_map/all_to_all | solution.py:39
  104.1 629.7 %all-to-all-done.1 = bf16[64,12,7168]{2,1,0:T(8,128)(2,1)} async-done(((bf16[64,12,7168]{2,1,0:T(8,128)(2,1)}), bf16[64,12,7168]{2,1,0:T(8,128)(2,1)}, u32[]{:S(2)}, u32[]{:S(2)}) %all-to-all-start.1) | async-done | bytes 11010080 | tf_op jit(solution)/shard_map/all_to_all | solution.py:39
  733.8 15.9 %reshape.81 = bf16[768,7168,1]{1,0,2:T(8,128)(2,1)} reshape(bf16[64,12,7168]{2,1,0:T(8,128)(2,1)} %all-to-all-done.1) | data formatting | bytes 22020096 | tf_op jit(solution)/shard_map/reshape | solution.py:44
  749.7 8.2 %multiply_reduce_fusion = (f32[2,768]{1,0:T(2,128)S(1)}, bf16[2,768,128]{1,2,0:T(8,128)(2,1)S(1)}) fusion(bf16[2,768,128]{1,2,0:T(8,128)(2,1)S(1)} %copy.62, f32[2,768]{1,0:T(2,128)S(1)} %bitcast.22, bf16[768,7168,1]{1,0,2:T(8,128)(2,1)} %reshape.81, bf16[2,128,7168]{2,1,0:T(8,128)(2,1)} %param.8), kind=kOutput, calls=%fused_computation.5 | convolution fusion | flops 2819553792 | bytes 15478784 | tf_op jit(solution)/shard_map/rd,ehd->erh/dot_general | solution.py:42
  758.0 23.9 %psum.7 = f32[64,12,2]{1,0,2:T(8,128)S(1)} all-reduce(f32[64,12,2]{1,0,2:T(8,128)S(1)} %reshape.69), channel_id=1, replica_groups=mesh['node'=64,'local'=8] {'local'}, use_global_device_ids=true, to_apply=%region_5.6 | all-reduce | flops 1536 | bytes 12288 | tf_op jit(solution)/shard_map/psum | solution.py:52
  782.0 0.7 copy.63
  782.6 17.3 %all-to-all-start.2 = ((f32[64,12,2]{1,2,0:T(2,128)}), f32[64,12,2]{1,2,0:T(2,128)S(1)}, u32[]{:S(2)}, u32[]{:S(2)}) async-start(f32[64,12,2]{1,2,0:T(2,128)} %copy.63), calls=%async_computation.2 | async-start | bytes 131072 | tf_op jit(solution)/shard_map/all_to_all | solution.py:53
  799.9 0.9 copy.66
  800.8 13.2 %all-to-all-done.2 = f32[64,12,2]{1,2,0:T(2,128)S(1)} async-done(((f32[64,12,2]{1,2,0:T(2,128)}), f32[64,12,2]{1,2,0:T(2,128)S(1)}, u32[]{:S(2)}, u32[]{:S(2)}) %all-to-all-start.2) | async-done | bytes 6176 | tf_op jit(solution)/shard_map/all_to_all | solution.py:53
  814.0 0.4 convolution_bitcast_fusion.1
  814.6 0.6 fusion.5
  815.2 0.7 copy.65
  (21 shorter events, 1.6 us)
Async XLA Ops:
  7.2 40.2 %all-gather.2.cloned.1.call-start = ((), (), s32[]{:S(2)}) async-start(), calls=%async_computation.3 | async-start | bytes 2064384 | tf_op jit(solution)/shard_map/all_gather | solution.py:36
  11.8 75.8 %all-to-all-start = ((bf16[64,12,2]{1,2,0:T(2,128)(2,1)}), bf16[64,12,2]{1,2,0:T(2,128)(2,1)S(1)}, u32[]{:S(2)}, u32[]{:S(2)}) async-start(bf16[64,12,2]{1,2,0:T(2,128)(2,1)} %convolution_convert_fusion), calls=%async_computation | async-start | bytes 65536 | tf_op jit(solution)/shard_map/all_to_all | solution.py:40
  87.5 16.0 %copy-start = (bf16[2,768,128]{2,1,0:T(8,128)(2,1)S(1)}, bf16[2,768,128]{2,1,0:T(8,128)(2,1)}, u32[]{:S(2)}) copy-start(bf16[2,768,128]{2,1,0:T(8,128)(2,1)} %param.9) | copy-start | bytes 1179652
  87.5 646.2 %all-to-all-start.1 = ((bf16[64,12,7168]{2,1,0:T(8,128)(2,1)}), bf16[64,12,7168]{2,1,0:T(8,128)(2,1)}, u32[]{:S(2)}, u32[]{:S(2)}) async-start(bf16[64,12,7168]{2,1,0:T(8,128)(2,1)} %broadcast_select_fusion), calls=%async_computation.1 | async-start | bytes 29360128 | tf_op jit(solution)/shard_map/all_to_all | solution.py:39
  782.6 31.4 %all-to-all-start.2 = ((f32[64,12,2]{1,2,0:T(2,128)}), f32[64,12,2]{1,2,0:T(2,128)S(1)}, u32[]{:S(2)}, u32[]{:S(2)}) async-start(f32[64,12,2]{1,2,0:T(2,128)} %copy.63), calls=%async_computation.2 | async-start | bytes 131072 | tf_op jit(solution)/shard_map/all_to_all | solution.py:53
Sparse Core Ops, SparseCore 0:
  10.1 37.2 all-gather.1
where the time goes:
time: 824 us; the launch traced here: 823 us
  waiting for transfers between devices  658 us (80%)
  starting transfers between devices  51.9 us (6%)
  local copies, waits for them, and re-layouts  47.3 us (6%)
  blocking collectives  23.9 us (3%)
  other arithmetic  16.3 us (2%)
  between operations  14.2 us (2%)
  matrix products  10.8 us (1%)
    all_to_all x1, waiting for transfers between devices, on_device(): lax.all_to_all(rows_send, 'node', split_axis=0, concat_axis=0, tiled=True)  630 us
    gather x2, local copies, waits for them, and re-layouts, gather_slots(): return jnp.take(padded, index, axis=0)  24.8 us
    psum x1, blocking collectives, on_device(): summed = lax.psum(partial_value, 'local')  23.9 us
    all_to_all x1, starting transfers between devices, on_device(): lax.all_to_all(prob_send, 'node', split_axis=0, concat_axis=0, tiled=True)  18.6 us
    all_to_all x1, starting transfers between devices, on_device(): lax.all_to_all(summed, 'node', split_axis=0, concat_axis=0, tiled=True)  17.3 us
  transfers between devices with their start and end apart: 4, of which 3 were waited for; matrix products, arithmetic and copies ran while one was open for 6% of the time, Pallas kernels for 0%

commit v1 on v0

--- a/solution.py
+++ b/solution.py
@@ -49,7 +49,7 @@
     grad_hidden = (scales[:, :, None] * hidden_grads).astype(jnp.bfloat16)
     partial_value = jnp.sum(saved_hidden.astype(jnp.float32) * hidden_grads, axis=2)
     partial_value = jnp.transpose(partial_value).reshape(node_count, capacity, expert_count)
-    summed = lax.psum(partial_value, "local")
+    summed = jnp.sum(lax.all_gather(partial_value, "local"), axis=0)
     returned = lax.all_to_all(summed, "node", split_axis=0, concat_axis=0, tiled=True)
     per_node = jnp.einsum("tms,msc->tmc", select_full, returned, precision=lax.Precision.HIGHEST)
     grad_probs = jnp.einsum("tjm,tmc->tjc", listed, per_node, precision=lax.Precision.HIGHEST)

time: 824 us -> 814 us (0.988)
  the two profiles are of different devices: /device:TPU:2 before, /device:TPU:1 now
where the time goes in v1:
time: 814 us; the launch traced here: 813 us
  waiting for transfers between devices  656 us (81%)
  starting transfers between devices  49.7 us (6%)
  local copies, waits for them, and re-layouts  47.5 us (6%)
  blocking collectives  18 us (2%)
  other arithmetic  16.4 us (2%)
  between operations  14.2 us (2%)
  matrix products  10.8 us (1%)
    all_to_all x1, waiting for transfers between devices, on_device(): lax.all_to_all(rows_send, 'node', split_axis=0, concat_axis=0, tiled=True)  627 us
    gather x2, local copies, waits for them, and re-layouts, gather_slots(): return jnp.take(padded, index, axis=0)  24.8 us
    all_to_all x1, starting transfers between devices, on_device(): lax.all_to_all(prob_send, 'node', split_axis=0, concat_axis=0, tiled=True)  19.1 us
    all_gather x1, blocking collectives, on_device(): summed = jnp.sum(lax.all_gather(partial_value, 'local'), axis=0)  18 us
  transfers between devices with their start and end apart: 4, of which 3 were waited for; matrix products, arithmetic and copies ran while one was open for 6% of the time, Pallas kernels for 0%

profile of v1, /device:TPU:1, one launch (start us, length us, event | category | flops | bytes accessed | tf_op | source)
XLA Modules:
  0.0 812.7 jit_solution(2798319504474610641)
XLA Ops:
  7.2 0.7 all-gather.2.cloned.1.call-update
  7.9 0.8 copy.61
  9.3 0.8 copy.64
  10.1 0.3 fusion.6
  10.6 1.2 convolution_convert_fusion
  11.8 19.1 %all-to-all-start = ((bf16[64,12,2]{1,2,0:T(2,128)(2,1)}), bf16[64,12,2]{1,2,0:T(2,128)(2,1)S(1)}, u32[]{:S(2)}, u32[]{:S(2)}) async-start(bf16[64,12,2]{1,2,0:T(2,128)(2,1)} %convolution_convert_fusion), calls=%async_computation | async-start | bytes 65536 | tf_op jit(solution)/shard_map/all_to_all | solution.py:40
  30.9 2.2 convert_reduce_fusion
  33.3 15.3 %all-gather.2.cloned.1.call-done = bf16[128,7168]{1,0:T(8,128)(2,1)} async-done(((bf16[128,896]{1,0:T(8,128)(2,1)}), bf16[128,7168]{1,0:T(8,128)(2,1)}) %all-gather.2.cloned.1.call-update) | async-done | bytes 1835024 | tf_op jit(solution)/shard_map/all_gather | solution.py:36
  48.5 1.7 concatenate.3
  50.2 9.5 %gather_fusion = bf16[768,7168]{1,0:T(8,128)(2,1)} fusion(bf16[129,7168]{1,0:T(8,128)(2,1)S(1)} %concatenate.3, s32[1024]{0:T(1024)S(1)} %pad_clamp_fusion), kind=kCustom, calls=%fused_computation | custom fusion | bytes 22023168 | tf_op jit(solution)/shard_map/jit(_take)/gather | solution.py:10
  59.7 15.4 %reshape.69 = bf16[64,12,7168]{2,1,0:T(8,128)(2,1)} reshape(bf16[768,7168]{1,0:T(8,128)(2,1)} %gather_fusion) | data formatting | bytes 22020096 | tf_op jit(solution)/shard_map/jit(_take)/gather | solution.py:10
  75.0 13.6 %broadcast_select_fusion = bf16[64,12,7168]{2,1,0:T(8,128)(2,1)} fusion(bf16[64,12,7168]{2,1,0:T(8,128)(2,1)} %reshape.69, pred[64,12]{1,0:T(8,128)(4,1)S(1)} %compare_and_fusion), kind=kLoop, calls=%fused_computation.1 | loop fusion | flops 5505024 | bytes 22020864 | tf_op jit(solution)/shard_map/jit(_take)/select_n | solution.py:10
  88.7 15.8 %all-to-all-start.1 = ((bf16[64,12,7168]{2,1,0:T(8,128)(2,1)}), bf16[64,12,7168]{2,1,0:T(8,128)(2,1)}, u32[]{:S(2)}, u32[]{:S(2)}) async-start(bf16[64,12,7168]{2,1,0:T(8,128)(2,1)} %broadcast_select_fusion), calls=%async_computation.1 | async-start | bytes 29360128 | tf_op jit(solution)/shard_map/all_to_all | solution.py:39
  105.0 627.0 %all-to-all-done.1 = bf16[64,12,7168]{2,1,0:T(8,128)(2,1)} async-done(((bf16[64,12,7168]{2,1,0:T(8,128)(2,1)}), bf16[64,12,7168]{2,1,0:T(8,128)(2,1)}, u32[]{:S(2)}, u32[]{:S(2)}) %all-to-all-start.1) | async-done | bytes 11010080 | tf_op jit(solution)/shard_map/all_to_all | solution.py:39
  732.0 15.9 %reshape.77 = bf16[768,7168,1]{1,0,2:T(8,128)(2,1)} reshape(bf16[64,12,7168]{2,1,0:T(8,128)(2,1)} %all-to-all-done.1) | data formatting | bytes 22020096 | tf_op jit(solution)/shard_map/reshape | solution.py:44
  747.9 8.2 %multiply_reduce_fusion = (f32[2,768]{1,0:T(2,128)S(1)}, bf16[2,768,128]{1,2,0:T(8,128)(2,1)S(1)}) fusion(bf16[2,768,128]{1,2,0:T(8,128)(2,1)S(1)} %copy.68, f32[2,768]{1,0:T(2,128)S(1)} %bitcast.22, bf16[768,7168,1]{1,0,2:T(8,128)(2,1)} %reshape.77, bf16[2,128,7168]{2,1,0:T(8,128)(2,1)} %param.8), kind=kOutput, calls=%fused_computation.5 | convolution fusion | flops 2819553792 | bytes 15478784 | tf_op jit(solution)/shard_map/rd,ehd->erh/dot_general | solution.py:42
  756.4 18.0 %all_gather.7 = f32[8,64,12,2]{1,3,2,0:T(2,128)S(1)} all-gather(f32[1,64,12,2]{1,3,2,0:T(2,128)S(1)} %copy.69), channel_id=1, replica_groups=mesh['node'=64,'local'=8] {'local'}, dimensions={0}, use_global_device_ids=true | all-gather | bytes 55296 | tf_op jit(solution)/shard_map/all_gather | solution.py:52
  774.4 0.7 copy.71
  775.2 14.7 %all-to-all-start.2 = ((f32[64,12,2]{1,2,0:T(2,128)}), f32[64,12,2]{1,2,0:T(2,128)S(1)}, u32[]{:S(2)}, u32[]{:S(2)}) async-start(f32[64,12,2]{1,2,0:T(2,128)} %copy.71), calls=%async_computation.2 | async-start | bytes 131072 | tf_op jit(solution)/shard_map/all_to_all | solution.py:53
  789.8 0.9 copy.74
  790.8 13.2 %all-to-all-done.2 = f32[64,12,2]{1,2,0:T(2,128)S(1)} async-done(((f32[64,12,2]{1,2,0:T(2,128)}), f32[64,12,2]{1,2,0:T(2,128)S(1)}, u32[]{:S(2)}, u32[]{:S(2)}) %all-to-all-start.2) | async-done | bytes 6176 | tf_op jit(solution)/shard_map/all_to_all | solution.py:53
  804.0 0.4 convolution_bitcast_fusion.1
  804.6 0.6 fusion.5
  805.2 0.7 copy.73
  (23 shorter events, 1.7 us)
Async XLA Ops:
  7.2 41.4 %all-gather.2.cloned.1.call-start = ((), (), s32[]{:S(2)}) async-start(), calls=%async_computation.3 | async-start | bytes 2064384 | tf_op jit(solution)/shard_map/all_gather | solution.py:36
  11.8 76.9 %all-to-all-start = ((bf16[64,12,2]{1,2,0:T(2,128)(2,1)}), bf16[64,12,2]{1,2,0:T(2,128)(2,1)S(1)}, u32[]{:S(2)}, u32[]{:S(2)}) async-start(bf16[64,12,2]{1,2,0:T(2,128)(2,1)} %convolution_convert_fusion), calls=%async_computation | async-start | bytes 65536 | tf_op jit(solution)/shard_map/all_to_all | solution.py:40
  88.7 15.8 %copy-start = (bf16[2,768,128]{2,1,0:T(8,128)(2,1)S(1)}, bf16[2,768,128]{2,1,0:T(8,128)(2,1)}, u32[]{:S(2)}) copy-start(bf16[2,768,128]{2,1,0:T(8,128)(2,1)} %param.9) | copy-start | bytes 1179652
  88.7 643.4 %all-to-all-start.1 = ((bf16[64,12,7168]{2,1,0:T(8,128)(2,1)}), bf16[64,12,7168]{2,1,0:T(8,128)(2,1)}, u32[]{:S(2)}, u32[]{:S(2)}) async-start(bf16[64,12,7168]{2,1,0:T(8,128)(2,1)} %broadcast_select_fusion), calls=%async_computation.1 | async-start | bytes 29360128 | tf_op jit(solution)/shard_map/all_to_all | solution.py:39
  775.2 28.8 %all-to-all-start.2 = ((f32[64,12,2]{1,2,0:T(2,128)}), f32[64,12,2]{1,2,0:T(2,128)S(1)}, u32[]{:S(2)}, u32[]{:S(2)}) async-start(f32[64,12,2]{1,2,0:T(2,128)} %copy.71), calls=%async_computation.2 | async-start | bytes 131072 | tf_op jit(solution)/shard_map/all_to_all | solution.py:53
Sparse Core Ops, SparseCore 0:
  10.1 38.3 all-gather.1
